TPU v7x, 128 devices: a whole 4x4x4 slice. The times are simulated.
128 devices in a mesh: rep: 4 (over x), fsdp: 2 (over core), tp: 16 (over z, y).
Axes of the slice: x: 4, y: 4, z: 4, core: 2. Of those that a mesh axis runs over, the one named last changes fastest.
Arguments:
- tokens: bfloat16 [8192, 2048], P(('rep', 'fsdp'), 'tp'), may hold values from -6 to 6
- cotangent: bfloat16 [8192, 2048], P(('rep', 'fsdp'), 'tp'), may hold values from -6 to 6
- frame_mask: int32 [8192], P(('rep', 'fsdp')), may hold values 0 or 1
- ln_gain: bfloat16 [2048], P('tp'), may hold values from 0.099609375 to 1.8984375
- ln_bias: bfloat16 [2048], P('tp'), may hold values from -3 to 3
- weight_in: bfloat16 [2048, 8192], P('fsdp', 'tp'), may hold values from -0.1875 to 0.1875
- weight_out: bfloat16 [8192, 2048], P('tp', 'fsdp'), may hold values from -0.09375 to 0.09375
- blocks_in: int32 [16, 64], P('fsdp', 'tp'), may hold values 0 or 1
- blocks_out: int32 [64, 16], P('tp', 'fsdp'), may hold values 0 or 1
Outputs:
- block_out: bfloat16 [8192, 2048], P(('rep', 'fsdp'), 'tp')
- input_grad: bfloat16 [8192, 2048], P(('rep', 'fsdp'), 'tp')
- grad_in: float32 [2048, 8192], P('fsdp', 'tp')
- grad_out: float32 [8192, 2048], P('tp', 'fsdp')
- grad_gain: float32 [2048], P('tp')
- grad_bias: float32 [2048], P('tp')
All inputs are finite; a program needn't handle non-finite values. No bound on the sum of `frame_mask` or of `blocks_in` or of `blocks_out` on one device may be relied on, other than what follows from the above.
Results may differ from a plain program's by a relative error of at most 0.019.
Values may be sent and summed in bfloat16 or wider, within the bound.
No kernel may reach another device: no remote copies, remote signals or barrier semaphores. Data moves between devices by JAX's collectives and lax.ppermute only.
A program may use at most 128 MiB of HBM per device.

v0:
```python
from functools import partial
import jax
import jax.numpy as jnp
from jax import lax
from jax.sharding import PartitionSpec as P

BLK = 128


def apply_blocks(weight, blocks, kind):
    row_blocks, col_blocks = blocks.shape
    shaped = weight.reshape(row_blocks, BLK, col_blocks, BLK)
    keeper = blocks.astype(kind)[:, None, :, None]
    return (shaped * keeper).reshape(weight.shape)


def contract_rows(left, right):
    return lax.dot_general(
        left, right, (((0,), (0,)), ((), ())), preferred_element_type=jnp.float32
    )


def contract_cols(left, right):
    return lax.dot_general(
        left, right, (((1,), (1,)), ((), ())), preferred_element_type=jnp.float32
    )


def on_device(
    tokens, cotangent, frame_mask, ln_gain, ln_bias, weight_in, weight_out, blocks_in, blocks_out
):
    whole_rows, whole_grad, gain_full, bias_full = (
        lax.all_gather(tokens, "tp", axis=1, tiled=True),
        lax.all_gather(cotangent, "tp", axis=1, tiled=True),
        lax.all_gather(ln_gain, "tp", axis=0, tiled=True),
        lax.all_gather(ln_bias, "tp", axis=0, tiled=True),
    )
    masked_in = apply_blocks(weight_in, blocks_in, jnp.bfloat16)
    masked_out = apply_blocks(weight_out, blocks_out, jnp.bfloat16)
    full_in, full_out = (
        lax.all_gather(masked_in, "fsdp", axis=0, tiled=True),
        lax.all_gather(masked_out, "fsdp", axis=1, tiled=True),
    )
    width = whole_rows.shape[1]
    own_width = tokens.shape[1]
    col_start = lax.axis_index("tp") * own_width
    gelu_exact = partial(jax.nn.gelu, approximate=False)
    values = whole_rows.astype(jnp.float32)
    centre = jnp.mean(values, axis=1, keepdims=True)
    centred = values - centre
    inv_std = lax.rsqrt(jnp.mean(centred * centred, axis=1, keepdims=True) + 1e-05)
    normed = centred * inv_std
    scaled = (normed * gain_full.astype(jnp.float32) + bias_full.astype(jnp.float32)).astype(
        jnp.bfloat16
    )
    hidden = jnp.dot(scaled, full_in, preferred_element_type=jnp.float32)
    active = gelu_exact(hidden).astype(jnp.bfloat16)
    partial_out = jnp.dot(active, full_out, preferred_element_type=jnp.float32)
    branch = lax.psum_scatter(
        partial_out.astype(jnp.bfloat16), "tp", scatter_dimension=1, tiled=True
    ).astype(jnp.float32)
    block_out = (tokens.astype(jnp.float32) + branch).astype(jnp.bfloat16)
    flags = frame_mask[:, None].astype(jnp.bfloat16)
    chosen = whole_grad * flags
    chosen_own = cotangent * flags
    back_active = contract_cols(chosen, full_out)
    unused, gelu_back = jax.vjp(gelu_exact, hidden)
    back_hidden = gelu_back(back_active)[0].astype(jnp.bfloat16)
    partial_normed = contract_cols(back_hidden, full_in)
    normed_own = lax.dynamic_slice_in_dim(normed, col_start, own_width, 1)
    gain_own = ln_gain.astype(jnp.float32)
    back_normed = lax.psum_scatter(
        partial_normed.astype(jnp.bfloat16), "tp", scatter_dimension=1, tiled=True
    ).astype(jnp.float32)
    back_scaled = back_normed * gain_own
    sum_plain = jnp.sum(back_scaled, axis=1)
    sum_cross = jnp.sum(back_scaled * normed_own, axis=1)
    sum_plain, sum_cross = lax.psum((sum_plain, sum_cross), "tp")
    mean_plain = (sum_plain / width)[:, None]
    mean_cross = (sum_cross / width)[:, None]
    back_rows = inv_std * (back_scaled - mean_plain - normed_own * mean_cross)
    input_grad = (chosen_own.astype(jnp.float32) + back_rows).astype(jnp.bfloat16)
    local_gain = jnp.sum(back_normed * normed_own, axis=0)
    local_bias = jnp.sum(back_normed, axis=0)
    grad_gain, grad_bias = lax.psum((local_gain, local_bias), ("rep", "fsdp"))
    term_in = contract_rows(scaled, back_hidden)
    term_out = contract_rows(active, chosen)
    shard_in, shard_out = (
        lax.psum_scatter(
            term_in.astype(jnp.bfloat16), "fsdp", scatter_dimension=0, tiled=True
        ).astype(jnp.float32),
        lax.psum_scatter(
            term_out.astype(jnp.bfloat16), "fsdp", scatter_dimension=1, tiled=True
        ).astype(jnp.float32),
    )
    shard_in, shard_out = (
        lax.psum(shard_in.astype(jnp.bfloat16), "rep").astype(jnp.float32),
        lax.psum(shard_out.astype(jnp.bfloat16), "rep").astype(jnp.float32),
    )
    grad_in = apply_blocks(shard_in, blocks_in, jnp.float32)
    grad_out = apply_blocks(shard_out, blocks_out, jnp.float32)
    return (block_out, input_grad, grad_in, grad_out, grad_gain, grad_bias)


def solution(mesh):
    placed = (
        P(("rep", "fsdp"), "tp"),
        P(("rep", "fsdp"), "tp"),
        P(("rep", "fsdp")),
        P("tp"),
        P("tp"),
        P("fsdp", "tp"),
        P("tp", "fsdp"),
        P("fsdp", "tp"),
        P("tp", "fsdp"),
    )
    return jax.shard_map(
        on_device,
        mesh=mesh,
        in_specs=placed,
        out_specs=(
            P(("rep", "fsdp"), "tp"),
            P(("rep", "fsdp"), "tp"),
            P("fsdp", "tp"),
            P("tp", "fsdp"),
            P("tp"),
            P("tp"),
        ),
        check_vma=False,
    )
```

profile of v0, /device:TPU:0, one launch (start us, length us, event | category | flops | bytes accessed | tf_op | source)
XLA Modules:
  0.0 492.1 jit_solution(3719068611543885792)
XLA Ops:
  7.2 0.0 all-gather.7.cloned.1.call-start
  7.2 0.7 all-gather.7.cloned.1.call-update
  7.9 0.0 all-gather.9.cloned.1.call-start
  7.9 0.8 fusion.34
  8.7 0.1 copy.17
  8.8 0.3 mul.149
  9.2 0.0 copy-start.2
  9.2 2.4 bitcast_multiply_fusion.3
  11.6 0.0 all-gather.9.cloned.1.call-update
  11.6 0.0 all-gather.11.cloned.1.call-start
  11.7 0.2 mul.155
  12.0 1.2 bitcast_multiply_fusion.2
  13.2 0.0 all-gather.11.cloned.1.call-update
  13.2 0.0 all-gather.13.cloned.1.call-start
  13.2 0.5 all-gather.13.cloned.1.call-update
  13.8 0.0 reduce-scatter.9.cloned.1.call-start
  13.8 22.1 %all-gather = bf16[16,1,128]{2,1,0:T(2,128)(2,1)S(1)} all-gather(bf16[1,1,128]{2,1,0:T(2,128)(2,1)S(1)} %bitcast.45), channel_id=1, replica_groups=mesh['rep'=4,'fsdp'=2,'tp'=16] {'tp'}, dimensions={0}, use_global_device_ids=true | all-gather | bytes 4352 | tf_op jit(solution)/shard_map/all_gather | solution.py:35
  36.0 19.5 %all-gather.1 = bf16[16,1,128]{2,1,0:T(2,128)(2,1)S(1)} all-gather(bf16[1,1,128]{2,1,0:T(2,128)(2,1)S(1)} %bitcast.44), channel_id=1, replica_groups=mesh['rep'=4,'fsdp'=2,'tp'=16] {'tp'}, dimensions={0}, use_global_device_ids=true | all-gather | bytes 4352 | tf_op jit(solution)/shard_map/all_gather | solution.py:36
  55.5 14.8 %all-gather.7.cloned.1.call-done = bf16[1024,2048]{1,0:T(8,128)(2,1)} async-done(((bf16[1024,128]{1,0:T(8,128)(2,1)}), bf16[1024,2048]{1,0:T(8,128)(2,1)}) %all-gather.7.cloned.1.call-update) | async-done | bytes 4194320 | tf_op jit(solution)/shard_map/all_gather | solution.py:33
  70.4 3.0 convert_reduce_fusion
  73.4 0.5 copy-done
  73.8 1.2 fusion.2
  75.1 10.1 %all-gather.9.cloned.1.call-done = bf16[2048,512]{1,0:T(8,128)(2,1)} async-done(((bf16[1024,512]{1,0:T(8,128)(2,1)}), bf16[2048,512]{1,0:T(8,128)(2,1)}) %all-gather.9.cloned.1.call-update) | async-done | bytes 2097168 | tf_op jit(solution)/shard_map/all_gather | solution.py:41
  85.1 10.5 %multiply_convert_fusion = (bf16[1024,512]{1,0:T(8,128)(2,1)S(1)}, f32[1024,512]{1,0:T(8,128)}, f32[1024,512]{1,0:T(8,128)}) fusion(bf16[2048,512]{1,0:T(8,128)(2,1)} %all-gather.9.cloned.1.call-done, f32[2048]{0:T(1024)S(1)} %bitcast.42, f32[2048]{0:T(1024)S(1)} %bitcast.40, f32[1024]{0:T(1024)S(1)} %add_rsqrt_fusion, ...), kind=kOutput, calls=%fused_computation.21 | convolution fusion | flops 2194145280 | bytes 11558912 | tf_op jit(solution)/shard_map/dot_general | solution.py:56
  95.6 5.8 %all-gather.11.cloned.1.call-done = bf16[512,2048]{1,0:T(8,128)(2,1)} async-done(((bf16[512,1024]{1,0:T(8,128)(2,1)}), bf16[512,2048]{1,0:T(8,128)(2,1)}) %all-gather.11.cloned.1.call-update) | async-done | bytes 2097168 | tf_op jit(solution)/shard_map/all_gather | solution.py:42
  101.4 61.1 %all-gather.13.cloned.1.call-done = bf16[1024,2048]{1,0:T(8,128)(2,1)} async-done(((bf16[1024,128]{1,0:T(8,128)(2,1)}), bf16[1024,2048]{1,0:T(8,128)(2,1)}) %all-gather.13.cloned.1.call-update) | async-done | bytes 4194320 | tf_op jit(solution)/shard_map/all_gather | solution.py:34
  162.5 7.1 %add_convert_fusion.1 = bf16[1024,512]{1,0:T(8,128)(2,1)S(1)} fusion(f32[1024,512]{1,0:T(8,128)} %get-tuple-element.17, f32[1024,512]{1,0:T(8,128)} %get-tuple-element.22, bf16[512,2048]{1,0:T(8,128)(2,1)} %all-gather.11.cloned.1.call-done, bf16[1024,2048]{1,0:T(8,128)(2,1)} %all-gather.13.cloned.1.call-done, bf16[1024]{0:T(1024)(128)(2,1)S(1)} %convert_element_type.88), kind=kOutput, calls=%fused_computation.18 | convolution fusion | flops 2156920832 | bytes 11536384 | tf_op jit(solution)/shard_map/dot_general | solution.py:24
  169.7 1.0 copy-done.14
  170.7 4.4 convolution_convert_fusion.2
  175.1 0.0 reduce-scatter.9.cloned.1.call-update
  175.1 0.2 reduce-scatter.11.cloned.1.call-start
  175.4 6.0 %fusion.7 = bf16[512,2048]{1,0:T(8,128)(2,1)} fusion(bf16[1024,512]{1,0:T(8,128)(2,1)S(1)} %get-tuple-element.16, bf16[1024,2048]{1,0:T(8,128)(2,1)} %all-gather.13.cloned.1.call-done, bf16[1024]{0:T(1024)(128)(2,1)S(1)} %convert_element_type.88), kind=kOutput, calls=%fused_computation.14 | convolution fusion | flops 2150629376 | bytes 7342080 | tf_op jit(solution)/shard_map/dot_general | solution.py:18
  181.3 0.0 reduce-scatter.11.cloned.1.call-update
  181.4 0.0 all-reduce.5.cloned.1.call-start
  181.4 5.3 %reduce-scatter.9.cloned.1.call-done = bf16[1024,512]{1,0:T(8,128)(2,1)} async-done(((bf16[2048,512]{1,0:T(8,128)(2,1)}), bf16[1024,512]{1,0:T(8,128)(2,1)}) %reduce-scatter.9.cloned.1.call-update) | async-done | bytes 1048592 | tf_op jit(solution)/shard_map/reduce_scatter | solution.py:89
  186.7 16.6 %reduce-scatter.11.cloned.1.call-done = bf16[512,1024]{1,0:T(8,128)(2,1)} async-done(((bf16[512,2048]{1,0:T(8,128)(2,1)}), bf16[512,1024]{1,0:T(8,128)(2,1)}) %reduce-scatter.11.cloned.1.call-update) | async-done | bytes 1048592 | tf_op jit(solution)/shard_map/reduce_scatter | solution.py:92
  203.3 0.0 all-reduce.5.cloned.1.call-update
  203.3 0.0 reduce-scatter.15.cloned.1.call-start
  203.4 5.5 %convolution_convert_fusion = bf16[1024,2048]{1,0:T(8,128)(2,1)} fusion(bf16[1024,512]{1,0:T(8,128)(2,1)} %copy-done.14, bf16[2048,512]{1,0:T(8,128)(2,1)S(1)} %copy-done.11), kind=kOutput, calls=%fused_computation.6 | convolution fusion | flops 2149580800 | bytes 7340032 | tf_op jit(solution)/shard_map/dot_general | solution.py:24
  208.9 6.4 %copy.21 = bf16[1024,2048]{0,1:T(8,128)(2,1)} copy(bf16[1024,2048]{1,0:T(8,128)(2,1)} %convolution_convert_fusion) | data formatting | bytes 8388608
  215.3 0.0 reduce-scatter.15.cloned.1.call-update
  215.3 0.0 reduce-scatter.13.cloned.1.call-start
  215.4 1.6 copy-done.12
  217.0 5.5 %convolution_convert_fusion.1 = bf16[1024,2048]{1,0:T(8,128)(2,1)} fusion(bf16[1024,512]{1,0:T(8,128)(2,1)} %copy-done.13, bf16[512,2048]{1,0:T(8,128)(2,1)S(1)} %copy-done.12), kind=kOutput, calls=%fused_computation.7 | convolution fusion | flops 2149580800 | bytes 7340032 | tf_op jit(solution)/shard_map/dot_general | solution.py:58
  222.5 6.4 %copy.19 = bf16[1024,2048]{0,1:T(8,128)(2,1)} copy(bf16[1024,2048]{1,0:T(8,128)(2,1)} %convolution_convert_fusion.1) | data formatting | bytes 8388608
  228.9 0.0 reduce-scatter.13.cloned.1.call-update
  228.9 0.1 copy.18
  229.0 6.4 %fusion = f32[1024,2048]{1,0:T(8,128)} fusion(bf16[1024,2048]{1,0:T(8,128)(2,1)} %all-gather.7.cloned.1.call-done, f32[1024]{0:T(1024)S(1)} %add_rsqrt_fusion, f32[1024]{0:T(1024)S(1)} %broadcast_multiply_fusion.2), kind=kLoop, calls=%fused_computation.2 | loop fusion | flops 6291456 | bytes 12591104 | tf_op jit(solution)/shard_map/mul | solution.py:52
  235.4 30.6 %all-reduce.5.cloned.1.call-done = (bf16[1024,512]{1,0:T(8,128)(2,1)}, bf16[512,1024]{1,0:T(8,128)(2,1)}) async-done(((bf16[1024,512]{1,0:T(8,128)(2,1)}, bf16[512,1024]{1,0:T(8,128)(2,1)}), (bf16[1024,512]{1,0:T(8,128)(2,1)}, bf16[512,1024]{1,0:T(8,128)(2,1)})) %all-reduce.5.cloned.1.call-update) | async-done | bytes 2097168 | tf_op jit(solution)/shard_map/psum | solution.py:97
  266.0 0.3 mul.177
  266.4 0.9 copy-done.4
  267.3 1.7 bitcast_multiply_fusion.1
  268.9 0.2 mul.180
  269.1 1.0 copy-done.3
  270.2 2.0 bitcast_multiply_fusion
  272.2 75.3 %reduce-scatter.15.cloned.1.call-done = bf16[128,1024]{1,0:T(8,128)(2,1)} async-done(((bf16[2048,1024]{1,0:T(8,128)(2,1)}), bf16[128,1024]{1,0:T(8,128)(2,1)}) %reduce-scatter.15.cloned.1.call-update) | async-done | bytes 262160
  347.4 1.1 copy.22
  348.5 79.2 %reduce-scatter.13.cloned.1.call-done = bf16[128,1024]{1,0:T(8,128)(2,1)} async-done(((bf16[2048,1024]{1,0:T(8,128)(2,1)}), bf16[128,1024]{1,0:T(8,128)(2,1)}) %reduce-scatter.13.cloned.1.call-update) | async-done | bytes 262160
  427.7 1.1 copy.20
  428.8 0.8 add_convert_fusion.4
  429.6 1.4 fusion.29
  431.0 13.5 %all-reduce.1 = (f32[128]{0:T(128)}, f32[128]{0:T(128)}) all-reduce(f32[128]{0:T(128)S(1)} %get-tuple-element.6, f32[128]{0:T(128)S(1)} %get-tuple-element.9), channel_id=1, replica_groups=mesh['rep'=4,'fsdp'=2,'tp'=16] {'rep','fsdp'}, use_global_device_ids=true, to_apply=%region_13.0 | all-reduce | flops 256 | bytes 2048 | tf_op jit(solution)/shard_map/psum | solution.py:85
  444.5 38.7 %all-reduce = (f32[1024]{0:T(1024)S(1)}, f32[1024]{0:T(1024)S(1)}) all-reduce(f32[1024]{0:T(1024)S(1)} %get-tuple-element.7, f32[1024]{0:T(1024)S(1)} %get-tuple-element.8), channel_id=1, replica_groups=mesh['rep'=4,'fsdp'=2,'tp'=16] {'tp'}, use_global_device_ids=true, to_apply=%region_7.0 | all-reduce | flops 2048 | bytes 16384 | tf_op jit(solution)/shard_map/psum | solution.py:78
  483.2 2.4 fusion.27
  (32 shorter events, 0.1 us)
Async XLA Ops:
  7.2 63.2 %all-gather.7.cloned.1.call-start = ((), (), s32[]{:S(2)}) async-start(), calls=%async_computation.4 | async-start | bytes 4456448 | tf_op jit(solution)/shard_map/all_gather | solution.py:33
  7.9 77.2 %all-gather.9.cloned.1.call-start = ((), (), s32[]{:S(2)}) async-start(), calls=%async_computation.5 | async-start | bytes 3145728 | tf_op jit(solution)/shard_map/all_gather | solution.py:41
  9.2 2.5 copy-start.8
  9.2 2.7 copy-start.2
  11.6 89.8 %all-gather.11.cloned.1.call-start = ((), (), s32[]{:S(2)}) async-start(), calls=%async_computation.6 | async-start | bytes 3145728 | tf_op jit(solution)/shard_map/all_gather | solution.py:42
  11.9 1.9 copy-start.10
  11.9 24.1 %copy-start.9 = (bf16[128]{0:T(256)(128)(2,1)S(1)}, bf16[128]{0:T(256)(128)(2,1)}, u32[]{:S(2)}) copy-start(bf16[128]{0:T(256)(128)(2,1)} %param.13) | copy-start | bytes 772
  11.9 43.6 %copy-start.7 = (s32[1024]{0:T(1024)S(1)}, s32[1024]{0:T(1024)}, u32[]{:S(2)}) copy-start(s32[1024]{0:T(1024)} %param.11) | copy-start | bytes 12292
  13.2 149.3 %all-gather.13.cloned.1.call-start = ((), (), s32[]{:S(2)}) async-start(), calls=%async_computation.7 | async-start | bytes 4456448 | tf_op jit(solution)/shard_map/all_gather | solution.py:34
  13.8 173.0 %reduce-scatter.9.cloned.1.call-start = ((), (), s32[]{:S(2)}) async-start(), calls=%async_computation.8 | async-start | bytes 3145728 | tf_op jit(solution)/shard_map/reduce_scatter | solution.py:89
  70.4 3.4 copy-start
  95.6 79.8 %copy-start.13 = (bf16[1024,512]{1,0:T(8,128)(2,1)}, bf16[1024,512]{1,0:T(8,128)(2,1)S(1)}, u32[]{:S(2)}) copy-start(bf16[1024,512]{1,0:T(8,128)(2,1)S(1)} %get-tuple-element.16) | copy-start | bytes 3145732
  162.5 8.1 %copy-start.1 = (bf16[1024,2048]{1,0:T(8,128)(2,1)S(1)}, bf16[1024,2048]{1,0:T(8,128)(2,1)}, u32[]{:S(2)}) copy-start(bf16[1024,2048]{1,0:T(8,128)(2,1)} %all-gather.7.cloned.1.call-done) | copy-start | bytes 12582916
  169.6 1.0 copy-start.14
  175.1 28.2 %reduce-scatter.11.cloned.1.call-start = ((), (), s32[]{:S(2)}) async-start(), calls=%async_computation.9 | async-start | bytes 3145728 | tf_op jit(solution)/shard_map/reduce_scatter | solution.py:92
  181.3 22.1 %copy-start.11 = (bf16[2048,512]{1,0:T(8,128)(2,1)S(1)}, bf16[2048,512]{1,0:T(8,128)(2,1)}, u32[]{:S(2)}) copy-start(bf16[2048,512]{1,0:T(8,128)(2,1)} %all-gather.9.cloned.1.call-done) | copy-start | bytes 6291460
  181.4 84.7 %all-reduce.5.cloned.1.call-start = ((), (), s32[]{:S(2)}) async-start(), calls=%async_computation.12 | async-start | bytes 4194304 | tf_op jit(solution)/shard_map/psum | solution.py:97
  203.3 144.1 %reduce-scatter.15.cloned.1.call-start = ((), (), s32[]{:S(2)}) async-start(), calls=%async_computation.11 | async-start | bytes 4456448
  215.3 1.6 copy-start.12
  215.3 212.4 %reduce-scatter.13.cloned.1.call-start = ((), (), s32[]{:S(2)}) async-start(), calls=%async_computation.10 | async-start | bytes 4456448
  266.0 1.2 copy-start.4
  268.9 1.2 copy-start.3
  270.2 158.7 %copy-start.5 = (bf16[1024,128]{1,0:T(8,128)(2,1)S(1)}, bf16[1024,128]{1,0:T(8,128)(2,1)}, u32[]{:S(2)}) copy-start(bf16[1024,128]{1,0:T(8,128)(2,1)} %param.9) | copy-start | bytes 786436
  272.2 211.0 %copy-start.6 = (bf16[1024,128]{1,0:T(8,128)(2,1)S(1)}, bf16[1024,128]{1,0:T(8,128)(2,1)}, u32[]{:S(2)}) copy-start(bf16[1024,128]{1,0:T(8,128)(2,1)} %param.10) | copy-start | bytes 786436
Sparse Core Ops, SparseCore 0:
  10.1 60.2 all-gather.6
  72.6 12.4 all-gather.8
  86.8 14.6 all-gather.10
  103.4 59.0 all-gather.12
  175.2 11.4 reduce-scatter.8
  189.6 13.6 reduce-scatter.10
  205.8 60.2 all-reduce.4
  269.7 77.6 reduce-scatter.14
  350.8 76.9 reduce-scatter.12
where the time goes:
time: 493 us; the launch traced here: 492 us
  waiting for transfers between devices  300 us (61%)
  blocking collectives  93.8 us (19%)
  matrix products  39 us (8%)
  other arithmetic  23.2 us (5%)
  local copies, waits for them, and re-layouts  21.3 us (4%)
  between operations  14.1 us (3%)
    unnamed x11, waiting for transfers between devices  156 us
    all_gather x1, waiting for transfers between devices, on_device(): lax.all_gather(cotangent, 'tp', axis=1, tiled=True)  61.1 us
    psum x1, blocking collectives, on_device(): sum_plain, sum_cross = lax.psum((sum_plain, sum_cross), 'tp')  38.7 us
    psum x1, waiting for transfers between devices, on_device(): lax.psum(shard_in.astype(jnp.bfloat16), 'rep').astype(jnp.float32)  30.6 us
    all_gather x1, blocking collectives, on_device(): lax.all_gather(ln_gain, 'tp', axis=0, tiled=True)  22.1 us
    unnamed x34, local copies, waits for them, and re-layouts  20 us
    all_gather x1, blocking collectives, on_device(): lax.all_gather(ln_bias, 'tp', axis=0, tiled=True)  19.5 us
    reduce_scatter x1, waiting for transfers between devices, on_device(): lax.psum_scatter(term_out.astype(jnp.bfloat16), 'fsdp', scatter_dimension...  16.6 us
  transfers between devices with their start and end apart: 9, of which 9 were waited for; matrix products, arithmetic and copies ran while one was open for 12% of the time, Pallas kernels for 0%

commit v1 on v0

--- a/solution.py
+++ b/solution.py
@@ -5,6 +5,11 @@
 from jax.sharding import PartitionSpec as P
 
 BLK = 128
+
+
+def swapped_in(x, axis, d):
+    stack = jnp.stack([x] * lax.axis_size(axis))
+    return jnp.concatenate(lax.all_to_all(stack, axis, 0, 0), axis=d)
 
 
 def apply_blocks(weight, blocks, kind):
@@ -38,7 +43,7 @@
     masked_in = apply_blocks(weight_in, blocks_in, jnp.bfloat16)
     masked_out = apply_blocks(weight_out, blocks_out, jnp.bfloat16)
     full_in, full_out = (
-        lax.all_gather(masked_in, "fsdp", axis=0, tiled=True),
+        swapped_in(masked_in, "fsdp", 0),
         lax.all_gather(masked_out, "fsdp", axis=1, tiled=True),
     )
     width = whole_rows.shape[1]

time: 493 us -> 476 us (0.966)
  waiting for transfers between devices: 300 us -> 280 us
    all_gather x1 -> x0, waiting for transfers between devices: 10.1 us -> none  [on_device(): lax.all_gather(masked_in, 'fsdp', axis=0, tiled=True)]
    all_gather x1, waiting for transfers between devices: 5.84 us -> 0.01 us  [on_device(): lax.all_gather(masked_out, 'fsdp', axis=1, tiled=True)]
    unnamed x11 -> x10, waiting for transfers between devices: 156 us -> 155 us
    unnamed x34 -> x30, local copies, waits for them, and re-layouts: 20 us -> 19.6 us
  transfers between devices with their start and end apart: 9 -> 9, of which waited for: 9 -> 7; matrix products, arithmetic and copies ran while one was open for 12% -> 13% of each run, Pallas kernels for 0% -> 0%
where the time goes in v1:
time: 476 us; the launch traced here: 474 us
  waiting for transfers between devices  280 us (59%)
  blocking collectives  93.2 us (20%)
  matrix products  37.6 us (8%)
  other arithmetic  23.7 us (5%)
  local copies, waits for them, and re-layouts  20.8 us (4%)
  between operations  14.4 us (3%)
    unnamed x10, waiting for transfers between devices  155 us
    all_gather x1, waiting for transfers between devices, on_device(): lax.all_gather(cotangent, 'tp', axis=1, tiled=True)  60.9 us
    psum x1, blocking collectives, on_device(): sum_plain, sum_cross = lax.psum((sum_plain, sum_cross), 'tp')  38.7 us
    psum x1, waiting for transfers between devices, on_device(): lax.psum(shard_in.astype(jnp.bfloat16), 'rep').astype(jnp.float32)  31.8 us
    all_gather x1, blocking collectives, on_device(): lax.all_gather(ln_bias, 'tp', axis=0, tiled=True)  22.2 us
    unnamed x30, local copies, waits for them, and re-layouts  19.6 us
    all_gather x1, blocking collectives, on_device(): lax.all_gather(ln_gain, 'tp', axis=0, tiled=True)  19.5 us
    reduce_scatter x1, waiting for transfers between devices, on_device(): lax.psum_scatter(term_out.astype(jnp.bfloat16), 'fsdp', scatter_dimension...  16.6 us
  transfers between devices with their start and end apart: 9, of which 7 were waited for; matrix products, arithmetic and copies ran while one was open for 13% of the time, Pallas kernels for 0%

profile of v1, /device:TPU:0, one launch (start us, length us, event | category | flops | bytes accessed | tf_op | source)
XLA Modules:
  0.0 474.2 jit_solution(7285723251199019257)
XLA Ops:
  7.2 0.0 all-gather.6.cloned.1.call-start
  7.2 0.7 all-gather.6.cloned.1.call-update
  7.9 0.0 all-gather.8.cloned.1.call-start
  7.9 0.8 fusion.34
  8.7 0.2 mul.159
  8.9 0.0 copy-start.8
  8.9 0.0 copy-start.2
  8.9 2.4 bitcast_multiply_fusion.2
  11.4 0.0 all-gather.8.cloned.1.call-update
  11.4 0.0 all-gather.10.cloned.1.call-start
  11.5 0.7 all-gather.10.cloned.1.call-update
  12.2 0.1 copy.17
  12.3 0.3 mul.152
  12.6 0.2 fusion.21
  12.8 1.5 pad_maximum_fusion
  14.3 3.9 all-to-all-start
  18.2 0.0 reduce-scatter.9.cloned.1.call-start
  18.3 22.2 %all-gather.1 = bf16[16,1,128]{2,1,0:T(2,128)(2,1)S(1)} all-gather(bf16[1,1,128]{2,1,0:T(2,128)(2,1)S(1)} %bitcast.51), channel_id=1, replica_groups=mesh['rep'=4,'fsdp'=2,'tp'=16] {'tp'}, dimensions={0}, use_global_device_ids=true | all-gather | bytes 4352 | tf_op jit(solution)/shard_map/all_gather | solution.py:41
  40.4 19.5 %all-gather = bf16[16,1,128]{2,1,0:T(2,128)(2,1)S(1)} all-gather(bf16[1,1,128]{2,1,0:T(2,128)(2,1)S(1)} %bitcast.52), channel_id=1, replica_groups=mesh['rep'=4,'fsdp'=2,'tp'=16] {'tp'}, dimensions={0}, use_global_device_ids=true | all-gather | bytes 4352 | tf_op jit(solution)/shard_map/all_gather | solution.py:40
  60.0 10.4 %all-gather.6.cloned.1.call-done = bf16[1024,2048]{1,0:T(8,128)(2,1)} async-done(((bf16[1024,128]{1,0:T(8,128)(2,1)}), bf16[1024,2048]{1,0:T(8,128)(2,1)}) %all-gather.6.cloned.1.call-update) | async-done | bytes 4194320 | tf_op jit(solution)/shard_map/all_gather | solution.py:38
  70.4 3.0 convert_reduce_fusion
  73.4 0.5 copy-done
  73.8 1.2 fusion.2
  75.1 0.0 all-to-all-done
  75.1 9.8 %multiply_convert_fusion = (bf16[1024,512]{1,0:T(8,128)(2,1)S(1)}, f32[1024,512]{1,0:T(8,128)}, f32[1024,512]{1,0:T(8,128)}) fusion(bf16[2048,512]{1,0:T(8,128)(2,1)S(1)} %bitcast.43, f32[2048]{0:T(1024)S(1)} %bitcast.47, f32[2048]{0:T(1024)S(1)} %bitcast.49, f32[1024]{0:T(1024)S(1)} %add_rsqrt_fusion, f32[1024]{0:T(1024)S(1)} %broadcast_multiply_fusion.2, ...), kind=kOutput, calls=%fused_computation.22 | convolution fusion | flops 2194145280 | bytes 11558912 | tf_op jit(solution)/shard_map/dot_general | solution.py:61
  84.9 60.9 %all-gather.10.cloned.1.call-done = bf16[1024,2048]{1,0:T(8,128)(2,1)} async-done(((bf16[1024,128]{1,0:T(8,128)(2,1)}), bf16[1024,2048]{1,0:T(8,128)(2,1)}) %all-gather.10.cloned.1.call-update) | async-done | bytes 4194320 | tf_op jit(solution)/shard_map/all_gather | solution.py:39
  145.8 7.1 %add_convert_fusion.1 = bf16[1024,512]{1,0:T(8,128)(2,1)S(1)} fusion(f32[1024,512]{1,0:T(8,128)} %get-tuple-element.17, f32[1024,512]{1,0:T(8,128)} %get-tuple-element.22, bf16[512,2048]{1,0:T(8,128)(2,1)} %all-gather.8.cloned.1.call-done, bf16[1024,2048]{1,0:T(8,128)(2,1)} %all-gather.10.cloned.1.call-done, bf16[1024]{0:T(1024)(128)(2,1)S(1)} %convert_element_type.88), kind=kOutput, calls=%fused_computation.19 | convolution fusion | flops 2156920832 | bytes 11536384 | tf_op jit(solution)/shard_map/dot_general | solution.py:29
  152.9 1.0 copy-done.11
  153.9 4.5 convolution_convert_fusion.2
  158.4 0.0 reduce-scatter.9.cloned.1.call-update
  158.4 0.2 reduce-scatter.11.cloned.1.call-start
  158.6 6.0 %fusion.7 = bf16[512,2048]{1,0:T(8,128)(2,1)} fusion(bf16[1024,512]{1,0:T(8,128)(2,1)S(1)} %get-tuple-element.16, bf16[1024,2048]{1,0:T(8,128)(2,1)} %all-gather.10.cloned.1.call-done, bf16[1024]{0:T(1024)(128)(2,1)S(1)} %convert_element_type.88), kind=kOutput, calls=%fused_computation.14 | convolution fusion | flops 2150629376 | bytes 7342080 | tf_op jit(solution)/shard_map/dot_general | solution.py:23
  164.6 0.0 reduce-scatter.11.cloned.1.call-update
  164.6 0.0 all-reduce.5.cloned.1.call-start
  164.7 5.3 %reduce-scatter.9.cloned.1.call-done = bf16[1024,512]{1,0:T(8,128)(2,1)} async-done(((bf16[2048,512]{1,0:T(8,128)(2,1)}), bf16[1024,512]{1,0:T(8,128)(2,1)}) %reduce-scatter.9.cloned.1.call-update) | async-done | bytes 1048592 | tf_op jit(solution)/shard_map/reduce_scatter | solution.py:94
  170.0 16.6 %reduce-scatter.11.cloned.1.call-done = bf16[512,1024]{1,0:T(8,128)(2,1)} async-done(((bf16[512,2048]{1,0:T(8,128)(2,1)}), bf16[512,1024]{1,0:T(8,128)(2,1)}) %reduce-scatter.11.cloned.1.call-update) | async-done | bytes 1048592 | tf_op jit(solution)/shard_map/reduce_scatter | solution.py:97
  186.6 0.0 all-reduce.5.cloned.1.call-update
  186.6 0.0 reduce-scatter.13.cloned.1.call-start
  186.6 5.9 %convolution_convert_fusion.1 = bf16[1024,2048]{1,0:T(8,128)(2,1)} fusion(bf16[1024,512]{1,0:T(8,128)(2,1)S(1)} %get-tuple-element.16, bf16[512,2048]{1,0:T(8,128)(2,1)} %all-gather.8.cloned.1.call-done), kind=kOutput, calls=%fused_computation.7 | convolution fusion | flops 2149580800 | bytes 7340032 | tf_op jit(solution)/shard_map/dot_general | solution.py:63
  192.5 6.4 %copy.19 = bf16[1024,2048]{0,1:T(8,128)(2,1)} copy(bf16[1024,2048]{1,0:T(8,128)(2,1)} %convolution_convert_fusion.1) | data formatting | bytes 8388608
  198.9 0.0 reduce-scatter.13.cloned.1.call-update
  198.9 0.0 reduce-scatter.15.cloned.1.call-start
  198.9 1.2 copy-done.12
  200.1 4.3 convolution_convert_fusion
  204.4 6.4 %copy.21 = bf16[1024,2048]{0,1:T(8,128)(2,1)} copy(bf16[1024,2048]{1,0:T(8,128)(2,1)} %convolution_convert_fusion) | data formatting | bytes 8388608
  210.8 0.0 reduce-scatter.15.cloned.1.call-update
  210.9 0.1 copy.18
  211.0 6.4 %fusion = f32[1024,2048]{1,0:T(8,128)} fusion(bf16[1024,2048]{1,0:T(8,128)(2,1)} %all-gather.6.cloned.1.call-done, f32[1024]{0:T(1024)S(1)} %add_rsqrt_fusion, f32[1024]{0:T(1024)S(1)} %broadcast_multiply_fusion.2), kind=kLoop, calls=%fused_computation.2 | loop fusion | flops 6291456 | bytes 12591104 | tf_op jit(solution)/shard_map/mul | solution.py:57
  217.4 31.8 %all-reduce.5.cloned.1.call-done = (bf16[1024,512]{1,0:T(8,128)(2,1)}, bf16[512,1024]{1,0:T(8,128)(2,1)}) async-done(((bf16[1024,512]{1,0:T(8,128)(2,1)}, bf16[512,1024]{1,0:T(8,128)(2,1)}), (bf16[1024,512]{1,0:T(8,128)(2,1)}, bf16[512,1024]{1,0:T(8,128)(2,1)})) %all-reduce.5.cloned.1.call-update) | async-done | bytes 2097168 | tf_op jit(solution)/shard_map/psum | solution.py:102
  249.1 0.3 mul.181
  249.5 0.9 copy-done.4
  250.4 1.7 bitcast_multiply_fusion.1
  252.1 0.2 mul.184
  252.3 1.0 copy-done.3
  253.3 2.0 bitcast_multiply_fusion
  255.3 75.3 %reduce-scatter.13.cloned.1.call-done = bf16[128,1024]{1,0:T(8,128)(2,1)} async-done(((bf16[2048,1024]{1,0:T(8,128)(2,1)}), bf16[128,1024]{1,0:T(8,128)(2,1)}) %reduce-scatter.13.cloned.1.call-update) | async-done | bytes 262160
  330.5 1.1 copy.20
  331.7 0.8 add_convert_fusion.4
  332.4 78.4 %reduce-scatter.15.cloned.1.call-done = bf16[128,1024]{1,0:T(8,128)(2,1)} async-done(((bf16[2048,1024]{1,0:T(8,128)(2,1)}), bf16[128,1024]{1,0:T(8,128)(2,1)}) %reduce-scatter.15.cloned.1.call-update) | async-done | bytes 262160
  410.8 1.1 copy.22
  411.9 1.4 fusion.30
  413.3 38.7 %all-reduce = (f32[1024]{0:T(1024)S(1)}, f32[1024]{0:T(1024)S(1)}) all-reduce(f32[1024]{0:T(1024)S(1)} %get-tuple-element.7, f32[1024]{0:T(1024)S(1)} %get-tuple-element.8), channel_id=1, replica_groups=mesh['rep'=4,'fsdp'=2,'tp'=16] {'tp'}, use_global_device_ids=true, to_apply=%region_7.0 | all-reduce | flops 2048 | bytes 16384 | tf_op jit(solution)/shard_map/psum | solution.py:83
  452.1 2.4 fusion.28
  454.4 12.9 %all-reduce.1 = (f32[128]{0:T(128)}, f32[128]{0:T(128)}) all-reduce(f32[128]{0:T(128)S(1)} %get-tuple-element.6, f32[128]{0:T(128)S(1)} %get-tuple-element.9), channel_id=1, replica_groups=mesh['rep'=4,'fsdp'=2,'tp'=16] {'rep','fsdp'}, use_global_device_ids=true, to_apply=%region_13.0 | all-reduce | flops 256 | bytes 2048 | tf_op jit(solution)/shard_map/psum | solution.py:90
  (28 shorter events, 0.1 us)
Async XLA Ops:
  7.2 63.2 %all-gather.6.cloned.1.call-start = ((), (), s32[]{:S(2)}) async-start(), calls=%async_computation.5 | async-start | bytes 4456448 | tf_op jit(solution)/shard_map/all_gather | solution.py:38
  7.9 77.0 %all-gather.8.cloned.1.call-start = ((), (), s32[]{:S(2)}) async-start(), calls=%async_computation.6 | async-start | bytes 3145728 | tf_op jit(solution)/shard_map/all_gather | solution.py:47
  8.9 3.2 copy-start.8
  8.9 3.7 copy-start.2
  11.4 134.4 %all-gather.10.cloned.1.call-start = ((), (), s32[]{:S(2)}) async-start(), calls=%async_computation.7 | async-start | bytes 4456448 | tf_op jit(solution)/shard_map/all_gather | solution.py:39
  14.3 4.0 copy-start.9
  14.3 26.1 %copy-start.10 = (bf16[128]{0:T(256)(128)(2,1)S(1)}, bf16[128]{0:T(256)(128)(2,1)}, u32[]{:S(2)}) copy-start(bf16[128]{0:T(256)(128)(2,1)} %param.12) | copy-start | bytes 772
  14.3 45.7 %copy-start.7 = (s32[1024]{0:T(1024)S(1)}, s32[1024]{0:T(1024)}, u32[]{:S(2)}) copy-start(s32[1024]{0:T(1024)} %param.11) | copy-start | bytes 12292
  14.3 60.8 %all-to-all-start = ((bf16[2,1024,512]{2,1,0:T(8,128)(2,1)}), bf16[2,1024,512]{2,1,0:T(8,128)(2,1)S(1)}, u32[]{:S(2)}, u32[]{:S(2)}) async-start(bf16[2,1024,512]{2,1,0:T(8,128)(2,1)} %pad_maximum_fusion), calls=%async_computation | async-start | bytes 4194304 | tf_op jit(solution)/shard_map/all_to_all | solution.py:12
  18.2 151.8 %reduce-scatter.9.cloned.1.call-start = ((), (), s32[]{:S(2)}) async-start(), calls=%async_computation.8 | async-start | bytes 3145728 | tf_op jit(solution)/shard_map/reduce_scatter | solution.py:94
  70.4 3.4 copy-start
  145.8 8.1 %copy-start.1 = (bf16[1024,2048]{1,0:T(8,128)(2,1)S(1)}, bf16[1024,2048]{1,0:T(8,128)(2,1)}, u32[]{:S(2)}) copy-start(bf16[1024,2048]{1,0:T(8,128)(2,1)} %all-gather.6.cloned.1.call-done) | copy-start | bytes 12582916
  152.9 1.0 copy-start.11
  158.4 28.2 %reduce-scatter.11.cloned.1.call-start = ((), (), s32[]{:S(2)}) async-start(), calls=%async_computation.9 | async-start | bytes 3145728 | tf_op jit(solution)/shard_map/reduce_scatter | solution.py:97
  164.6 84.5 %all-reduce.5.cloned.1.call-start = ((), (), s32[]{:S(2)}) async-start(), calls=%async_computation.12 | async-start | bytes 4194304 | tf_op jit(solution)/shard_map/psum | solution.py:102
  186.6 143.9 %reduce-scatter.13.cloned.1.call-start = ((), (), s32[]{:S(2)}) async-start(), calls=%async_computation.10 | async-start | bytes 4456448
  198.9 1.2 copy-start.12
  198.9 211.9 %reduce-scatter.15.cloned.1.call-start = ((), (), s32[]{:S(2)}) async-start(), calls=%async_computation.11 | async-start | bytes 4456448
  249.1 1.2 copy-start.4
  252.1 1.2 copy-start.3
  253.3 78.4 %copy-start.5 = (bf16[1024,128]{1,0:T(8,128)(2,1)S(1)}, bf16[1024,128]{1,0:T(8,128)(2,1)}, u32[]{:S(2)}) copy-start(bf16[1024,128]{1,0:T(8,128)(2,1)} %param.9) | copy-start | bytes 786436
  255.3 196.8 %copy-start.6 = (bf16[1024,128]{1,0:T(8,128)(2,1)S(1)}, bf16[1024,128]{1,0:T(8,128)(2,1)}, u32[]{:S(2)}) copy-start(bf16[1024,128]{1,0:T(8,128)(2,1)} %param.10) | copy-start | bytes 786436
Sparse Core Ops, SparseCore 0:
  10.1 60.2 all-gather.5
  72.0 12.4 all-gather.7
  86.7 59.0 all-gather.9
  158.5 11.4 reduce-scatter.8
  172.9 13.6 reduce-scatter.10
  188.9 60.2 all-reduce.4
  252.8 77.6 reduce-scatter.12
  333.9 76.9 reduce-scatter.14
